TPU v7x, 32 devices: a whole 2x2x4 slice. The times are simulated.
32 devices in a mesh: dp: 8 (over y, x, core), space: 4 (over z).
Axes of the slice: x: 2, y: 2, z: 4, core: 2. Of those that a mesh axis runs over, the one named last changes fastest.
Arguments:
- volume: bfloat16 [8, 32, 8, 16, 128], P('dp', None, 'space')
- out_grad: bfloat16 [8, 32, 8, 16, 128], P('dp', None, 'space'), may hold values from -0.016479492 to 0.016479492
- kernel: bfloat16 [32, 864], replicated, may hold values from -0.21875 to 0.21875
- sample_idx: int32 [8, 4096], P('dp', 'space'), may hold values from 0 to 4095
- a_inverse: float32 [864, 864], P('space')
- g_inverse: float32 [32, 32], replicated
Outputs:
- conv_out: bfloat16 [8, 32, 8, 16, 128], P('dp', None, 'space')
- a_factor: float32 [864, 864], P('dp', 'space')
- g_factor: float32 [32, 32], replicated
- pre_grad: float32 [32, 864], replicated
Inputs may be any that keep to these rules, and one draw needn't show every extreme that they name: `sample_idx`: column s of a sample's row names a cell of slab s // 1024, as the number z * 16 * 128 + y * 128 + x counted within that slab of 2 planes.
All inputs are finite; a program needn't handle non-finite values.
Results may differ from a plain program's by a relative error of at most 0.0085.
Values may be sent and summed in bfloat16 or wider, within the bound.
No kernel may reach another device: no remote copies, remote signals or barrier semaphores. Data moves between devices by JAX's collectives and lax.ppermute only.
A program may use at most 128 MiB of HBM per device.

v0:
```python
import jax
import jax.numpy as jnp
from jax import lax
from jax.sharding import PartitionSpec as P


def padded_2(cells, sides, width):
    for axis, dim in sides:
        count = lax.axis_size(axis)
        ends = count - 1
        head = lax.slice_in_dim(cells, 0, width, axis=dim)
        tail = lax.slice_in_dim(cells, cells.shape[dim] - width, cells.shape[dim], axis=dim)
        cells = jnp.concatenate(
            [
                lax.ppermute(tail, axis, [(i, (i + 1) % count) for i in range(ends)]),
                cells,
                lax.ppermute(head, axis, [((i + 1) % count, i) for i in range(ends)]),
            ],
            axis=dim,
        )
    return cells


def on_device(volume, out_grad, kernel, sample_idx, a_inverse, g_inverse):
    highest = lax.Precision.HIGHEST
    f32 = jnp.float32
    channels = volume.shape[1]
    planes = volume.shape[2]
    y_cells = volume.shape[3]
    x_cells = volume.shape[4]
    cells = planes * y_cells * x_cells
    patch = kernel.shape[1]
    n_dp = lax.axis_size("dp")
    n_sp = lax.axis_size("space")
    contract_cells = (((1,), (1,)), ((), ()))
    block = padded_2(volume, (("space", 2),), 1)
    padded = jnp.pad(block[0], ((0, 0), (0, 0), (1, 1), (1, 1)))
    taps = [
        padded[:, dz : dz + planes, dy : dy + y_cells, dx : dx + x_cells]
        for dz in range(3)
        for dy in range(3)
        for dx in range(3)
    ]
    patches_t = jnp.stack(taps, axis=1).reshape(patch, cells)
    grad_flat = out_grad[0].reshape(channels, cells)
    forward = jnp.dot(kernel, patches_t, preferred_element_type=f32)
    conv_out = forward.astype(jnp.bfloat16).reshape(1, channels, planes, y_cells, x_cells)
    grad_w = lax.dot_general(grad_flat, patches_t, contract_cells, preferred_element_type=f32)
    g_part = lax.dot_general(grad_flat, grad_flat, contract_cells, preferred_element_type=f32)
    cell_ids = sample_idx[0]
    counts = jnp.sum(
        (cell_ids[:, None] == jnp.arange(cells, dtype=jnp.int32)[None, :]).astype(f32), axis=0
    )
    weighted = patches_t.astype(f32) * counts[None, :]
    high = weighted.astype(jnp.bfloat16)
    low = (weighted - high.astype(f32)).astype(jnp.bfloat16)
    total_samples = sample_idx.shape[1] * n_sp * n_dp
    a_part = (
        lax.dot_general(high, patches_t, contract_cells, preferred_element_type=f32)
        + lax.dot_general(low, patches_t, contract_cells, preferred_element_type=f32)
    ) / jnp.float32(total_samples)
    rows = patch // n_dp
    cols = patch // n_sp
    a_blocks = (
        a_part.astype(jnp.bfloat16)
        .reshape(n_dp, rows, n_sp, cols)
        .transpose(0, 2, 1, 3)
        .reshape(n_dp * n_sp, rows, cols)
    )
    a_factor = lax.psum_scatter(a_blocks, ("dp", "space"), scatter_dimension=0, tiled=True)
    a_factor = a_factor.reshape(rows, cols).astype(f32)
    both = lax.psum(jnp.concatenate([grad_w, g_part], axis=1), ("dp", "space"))
    grad_sum = both[:, :patch]
    g_factor = both[:, patch:]
    left = jnp.dot(g_inverse, grad_sum, precision=highest)
    own_rows = a_inverse.shape[0]
    left_rows = lax.dynamic_slice_in_dim(left, lax.axis_index("space") * own_rows, own_rows, axis=1)
    pre_grad = lax.psum(jnp.dot(left_rows, a_inverse, precision=highest), "space")
    return (conv_out, a_factor, g_factor, pre_grad)


def solution(mesh):
    placed = (
        P("dp", None, "space", None, None),
        P("dp", None, "space", None, None),
        P(),
        P("dp", "space"),
        P("space", None),
        P(),
    )
    return jax.shard_map(
        on_device,
        mesh=mesh,
        in_specs=placed,
        out_specs=(P("dp", None, "space", None, None), P("dp", "space"), P(), P()),
        check_vma=False,
    )
```

profile of v0, /device:TPU:0, one launch (start us, length us, event | category | flops | bytes accessed | tf_op | source)
XLA Modules:
  0.0 373.9 jit_solution(7109457592317233880)
XLA Ops:
  8.3 4.9 %collective-permute-start = (bf16[1,32,1,16,128]{4,3,2,1,0:T(8,128)(2,1)S(1)}, bf16[1,32,1,16,128]{4,3,2,1,0:T(8,128)(2,1)S(1)}, u32[]{:S(2)}, u32[]{:S(2)}) collective-permute-start(bf16[1,32,1,16,128]{4,3,2,1,0:T(8,128)(2,1)S(1)} %get-tuple-element.6), channel_id=1, source_target_pairs={{0,1},{1,2},{2,3},{4,5},{5,6},{6,7},{8,9},{9,10},{10,11},{12,13},{... | collective-permute-start | bytes 393224 | tf_op jit(solution)/shard_map/ppermute | solution.py:15
  13.2 1.3 collective-permute-start.1
  14.5 3.4 convert_reduce_fusion
  19.0 1.3 convolution_bitcast_fusion.1
  25.6 4.6 %copy.25 = bf16[32,27,2,16,128]{4,3,2,1,0:T(8,128)(2,1)} copy(bf16[32,27,2,16,128]{4,3,2,0,1:T(8,128)(2,1)S(1)} %fusion.49) | data formatting | bytes 14155776 | tf_op jit(solution)/shard_map/stack | solution.py:44
  30.8 12.0 %subtract_convert_fusion = (bf16[32,27,2,16,128]{4,3,2,0,1:T(8,128)(2,1)}, bf16[32,27,2,16,128]{4,3,2,0,1:T(8,128)(2,1)}) fusion(bf16[32,27,2,16,128]{4,3,2,0,1:T(8,128)(2,1)} %copy-done.1, f32[2,16,128]{2,1,0:T(8,128)S(1)} %bitcast.151), kind=kLoop, calls=%fused_computation.2 | loop fusion | flops 21233664 | bytes 21250048 | tf_op jit(solution)/shard_map/convert_element_type | solution.py:56
  42.9 7.1 %copy.26 = bf16[32,27,2,16,128]{4,3,2,1,0:T(8,128)(2,1)} copy(bf16[32,27,2,16,128]{4,3,2,0,1:T(8,128)(2,1)} %get-tuple-element.5) | data formatting | bytes 14155776 | tf_op jit(solution)/shard_map/convert_element_type | solution.py:55
  50.0 11.6 %convert_element_type.83 = bf16[864,4096]{1,0:T(8,128)(2,1)} reshape(bf16[32,27,2,16,128]{4,3,2,1,0:T(8,128)(2,1)} %copy.26) | data formatting | bytes 14155776 | tf_op jit(solution)/shard_map/convert_element_type | solution.py:55
  61.6 11.6 %reshape.94 = bf16[864,4096]{1,0:T(8,128)(2,1)} reshape(bf16[32,27,2,16,128]{4,3,2,1,0:T(8,128)(2,1)} %copy.25) | data formatting | bytes 14155776 | tf_op jit(solution)/shard_map/reshape | solution.py:44
  73.2 7.1 %copy.27 = bf16[32,27,2,16,128]{4,3,2,1,0:T(8,128)(2,1)} copy(bf16[32,27,2,16,128]{4,3,2,0,1:T(8,128)(2,1)} %get-tuple-element.4) | data formatting | bytes 14155776 | tf_op jit(solution)/shard_map/convert_element_type | solution.py:56
  80.3 11.6 %convert_element_type.86 = bf16[864,4096]{1,0:T(8,128)(2,1)} reshape(bf16[32,27,2,16,128]{4,3,2,1,0:T(8,128)(2,1)} %copy.27) | data formatting | bytes 14155776 | tf_op jit(solution)/shard_map/convert_element_type | solution.py:56
  91.9 12.9 %fusion.60 = f32[864,864]{1,0:T(8,128)} fusion(bf16[864,4096]{1,0:T(8,128)(2,1)} %convert_element_type.83, bf16[864,4096]{1,0:T(8,128)(2,1)} %reshape.94), kind=kOutput, calls=%fused_computation.98 | convolution fusion | flops 6115295232 | bytes 17141760 | tf_op jit(solution)/shard_map/dot_general | solution.py:59
  104.8 5.1 %convolution_bitcast_fusion = f32[32,864]{1,0:T(8,128)S(1)} fusion(bf16[864,4096]{1,0:T(8,128)(2,1)} %reshape.94, bf16[32,4096]{1,0:T(8,128)(2,1)S(1)} %reshape_squeeze.3), kind=kOutput, calls=%fused_computation.32 | convolution fusion | flops 226492416 | bytes 7450624 | tf_op jit(solution)/shard_map/dot_general | solution.py:48
  110.7 13.3 %multiply_convert_fusion = bf16[864,864]{1,0:T(8,128)(2,1)} fusion(f32[864,864]{1,0:T(8,128)} %fusion.60, bf16[864,4096]{1,0:T(8,128)(2,1)} %convert_element_type.86, bf16[864,4096]{1,0:T(8,128)(2,1)} %reshape.94), kind=kOutput, calls=%fused_computation.30 | convolution fusion | flops 6117534720 | bytes 18634752 | tf_op jit(solution)/shard_map/dot_general | solution.py:60
  124.0 4.6 %reshape.96 = bf16[8,108,4,216]{3,2,1,0:T(4,128)(2,1)S(1)} reshape(bf16[864,864]{1,0:T(8,128)(2,1)} %multiply_convert_fusion) | data formatting | bytes 2985984 | tf_op jit(solution)/shard_map/reshape | solution.py:66
  128.6 2.6 copy.28
  131.2 4.4 %fusion.1 = bf16[4,8,32,128]{3,1,2,0:T(8,128)(2,1)S(1)} fusion(bf16[32,864]{1,0:T(8,128)(2,1)S(1)} %copy-done.2, bf16[864,4096]{1,0:T(8,128)(2,1)} %reshape.94), kind=kOutput, calls=%fused_computation.31 | convolution fusion | flops 226623488 | bytes 7395328 | tf_op jit(solution)/shard_map/dot_general | solution.py:46
  136.3 97.5 %all-reduce.5.cloned.1.call-done = f32[32,896]{1,0:T(8,128)} async-done(((f32[32,896]{1,0:T(8,128)}), f32[32,896]{1,0:T(8,128)}) %all-reduce.5.cloned.1.call-update) | async-done | bytes 114704 | tf_op jit(solution)/shard_map/psum | solution.py:72
  235.0 1.3 fusion.56
  236.3 1.4 slice.130
  237.7 92.0 %reduce-scatter.4.cloned.1.call-done = bf16[1,108,216]{1,2,0:T(8,128)(2,1)} async-done(((bf16[32,108,216]{1,2,0:T(8,128)(2,1)}), bf16[1,108,216]{1,2,0:T(8,128)(2,1)}) %reduce-scatter.4.cloned.1.call-update) | async-done | bytes 46672
  329.7 1.5 bitcast_convert_fusion
  331.2 34.7 %all-reduce.7.cloned.1.call-done = f32[32,864]{1,0:T(8,128)} async-done(((f32[32,864]{1,0:T(8,128)}), f32[32,864]{1,0:T(8,128)}) %all-reduce.7.cloned.1.call-update) | async-done | bytes 110608 | tf_op jit(solution)/shard_map/psum | solution.py:78
  365.9 1.6 copy.63
  (49 shorter events, 10.8 us)
Async XLA Ops:
  7.2 227.8 %copy-start = (f32[216,864]{1,0:T(8,128)S(1)}, f32[216,864]{1,0:T(8,128)}, u32[]{:S(2)}) copy-start(f32[216,864]{1,0:T(8,128)} %param.10) | copy-start | bytes 2239492
  7.2 226.7 %all-reduce.5.cloned.1.call-start = ((), (), s32[]{:S(2)}) async-start(), calls=%async_computation.1 | async-start | bytes 229376 | tf_op jit(solution)/shard_map/psum | solution.py:72
  8.3 12.0 %collective-permute-start = (bf16[1,32,1,16,128]{4,3,2,1,0:T(8,128)(2,1)S(1)}, bf16[1,32,1,16,128]{4,3,2,1,0:T(8,128)(2,1)S(1)}, u32[]{:S(2)}, u32[]{:S(2)}) collective-permute-start(bf16[1,32,1,16,128]{4,3,2,1,0:T(8,128)(2,1)S(1)} %get-tuple-element.6), channel_id=1, source_target_pairs={{0,1},{1,2},{2,3},{4,5},{5,6},{6,7},{8,9},{9,10},{10,11},{12,13},{... | collective-permute-start | bytes 393224 | tf_op jit(solution)/shard_map/ppermute | solution.py:15
  13.2 7.0 %collective-permute-start.1 = (bf16[1,32,1,16,128]{4,3,2,1,0:T(8,128)(2,1)S(1)}, bf16[1,32,1,16,128]{4,3,2,1,0:T(8,128)(2,1)S(1)}, u32[]{:S(2)}, u32[]{:S(2)}) collective-permute-start(bf16[1,32,1,16,128]{4,3,2,1,0:T(8,128)(2,1)S(1)} %get-tuple-element.7), channel_id=1, source_target_pairs={{1,0},{2,1},{3,2},{5,4},{6,5},{7,6},{9,8},{10,9},{11,10},{13,12},{... | collective-permute-start | bytes 393224 | tf_op jit(solution)/shard_map/ppermute | solution.py:17
  25.6 5.3 %copy-start.1 = (bf16[32,27,2,16,128]{4,3,2,0,1:T(8,128)(2,1)}, bf16[32,27,2,16,128]{4,3,2,0,1:T(8,128)(2,1)S(1)}, u32[]{:S(2)}) copy-start(bf16[32,27,2,16,128]{4,3,2,0,1:T(8,128)(2,1)S(1)} %fusion.49) | copy-start | bytes 21233668
  110.7 219.0 %reduce-scatter.4.cloned.1.call-start = ((), (), s32[]{:S(2)}) async-start(), calls=%async_computation.3 | async-start | bytes 1824768
  124.0 7.2 %copy-start.2 = (bf16[32,864]{1,0:T(8,128)(2,1)S(1)}, bf16[32,864]{1,0:T(8,128)(2,1)}, u32[]{:S(2)}) copy-start(bf16[32,864]{1,0:T(8,128)(2,1)} %param.8) | copy-start | bytes 165892
  128.5 105.3 %copy-start.3 = (f32[32,32]{1,0:T(8,128)S(1)}, f32[32,32]{1,0:T(8,128)}, u32[]{:S(2)}) copy-start(f32[32,32]{1,0:T(8,128)} %param.11) | copy-start | bytes 12292
  131.1 234.7 %all-reduce.7.cloned.1.call-start = ((), (), s32[]{:S(2)}) async-start(), calls=%async_computation.2 | async-start | bytes 229376 | tf_op jit(solution)/shard_map/psum | solution.py:78
Sparse Core Ops, SparseCore 0:
  110.8 123.0 all-reduce.4
  239.2 90.4 reduce-scatter.3
  332.7 33.1 all-reduce.6
where the time goes:
time: 375 us; the launch traced here: 374 us
  waiting for transfers between devices  224 us (60%)
  local copies, waits for them, and re-layouts  71.4 us (19%)
  matrix products  39.4 us (11%)
  other arithmetic  18.6 us (5%)
  between operations  14 us (4%)
  starting transfers between devices  6.35 us (2%)
    psum x1, waiting for transfers between devices, on_device(): both = lax.psum(jnp.concatenate([grad_w, g_part], axis=1), ('dp', 'space'))  97.5 us
    unnamed x4, waiting for transfers between devices  92 us
    psum x1, waiting for transfers between devices, on_device(): lax.psum(jnp.dot(left_rows, a_inverse, precision=highest), 'space')  34.7 us
    convert_element_type x2, local copies, waits for them, and re-layouts, on_device(): high = weighted.astype(jnp.bfloat16)  18.8 us
    convert_element_type x2, local copies, waits for them, and re-layouts, on_device(): low = (weighted - high.astype(f32)).astype(jnp.bfloat16)  18.6 us
    dot_general x1, matrix products, on_device(): lax.dot_general(low, patches_t, contract_cells, preferred_element_type=f32)  13.3 us
    dot_general x1, matrix products, on_device(): lax.dot_general(high, patches_t, contract_cells, preferred_element_type=f32)  12.9 us
    convert_element_type x1, other arithmetic, on_device(): low = (weighted - high.astype(f32)).astype(jnp.bfloat16)  12 us
  transfers between devices with their start and end apart: 5, of which 3 were waited for; matrix products, arithmetic and copies ran while one was open for 10% of the time, Pallas kernels for 0%

commit v1 on v0

--- a/solution.py
+++ b/solution.py
@@ -2,6 +2,8 @@
 import jax.numpy as jnp
 from jax import lax
 from jax.sharding import PartitionSpec as P
+
+run_edge_on = lambda vector: lax.psum(lax.psum(vector, axis_name="space"), axis_name="dp")
 
 
 def padded_2(cells, sides, width):
@@ -69,7 +71,7 @@
     )
     a_factor = lax.psum_scatter(a_blocks, ("dp", "space"), scatter_dimension=0, tiled=True)
     a_factor = a_factor.reshape(rows, cols).astype(f32)
-    both = lax.psum(jnp.concatenate([grad_w, g_part], axis=1), ("dp", "space"))
+    both = run_edge_on(jnp.concatenate([grad_w, g_part], axis=1))
     grad_sum = both[:, :patch]
     g_factor = both[:, patch:]
     left = jnp.dot(g_inverse, grad_sum, precision=highest)

time: 375 us -> 239 us (0.64)
  waiting for transfers between devices: 224 us -> 86.2 us
    psum x1 -> x2, waiting for transfers between devices: 97.5 us -> 34 us  [the longest x1 29 us: lax.psum(lax.psum(vector, axis_name='space'), axis_name='dp')]
    unnamed x4 -> x5, waiting for transfers between devices: 92 us -> 52.2 us
    psum x1, waiting for transfers between devices: 34.7 us -> 0.01 us  [on_device(): lax.psum(jnp.dot(left_rows, a_inverse, precision=highest), 'space')]
  transfers between devices with their start and end apart: 5 -> 6, of which waited for: 3 -> 3; matrix products, arithmetic and copies ran while one was open for 10% -> 29% of each run, Pallas kernels for 0% -> 0%
where the time goes in v1:
time: 239 us; the launch traced here: 237 us
  waiting for transfers between devices  86.2 us (36%)
  local copies, waits for them, and re-layouts  71.3 us (30%)
  matrix products  39.3 us (16%)
  other arithmetic  18.7 us (8%)
  between operations  15.4 us (6%)
  starting transfers between devices  6.39 us (3%)
    unnamed x5, waiting for transfers between devices  52.2 us
    psum x1, waiting for transfers between devices, lax.psum(lax.psum(vector, axis_name='space'), axis_name='dp')  29 us
    convert_element_type x2, local copies, waits for them, and re-layouts, on_device(): high = weighted.astype(jnp.bfloat16)  18.8 us
    convert_element_type x2, local copies, waits for them, and re-layouts, on_device(): low = (weighted - high.astype(f32)).astype(jnp.bfloat16)  18.6 us
    dot_general x1, matrix products, on_device(): lax.dot_general(low, patches_t, contract_cells, preferred_element_type=f32)  13.2 us
    dot_general x1, matrix products, on_device(): lax.dot_general(high, patches_t, contract_cells, preferred_element_type=f32)  12.9 us
    convert_element_type x1, other arithmetic, on_device(): low = (weighted - high.astype(f32)).astype(jnp.bfloat16)  12.1 us
    reshape x1, local copies, waits for them, and re-layouts, on_device(): patches_t = jnp.stack(taps, axis=1).reshape(patch, cells)  11.6 us
  transfers between devices with their start and end apart: 6, of which 3 were waited for; matrix products, arithmetic and copies ran while one was open for 29% of the time, Pallas kernels for 0%

profile of v1, /device:TPU:0, one launch (start us, length us, event | category | flops | bytes accessed | tf_op | source)
XLA Modules:
  0.0 237.4 jit_solution(1246254837047836308)
XLA Ops:
  9.1 4.9 %collective-permute-start = (bf16[1,32,1,16,128]{4,3,2,1,0:T(8,128)(2,1)S(1)}, bf16[1,32,1,16,128]{4,3,2,1,0:T(8,128)(2,1)S(1)}, u32[]{:S(2)}, u32[]{:S(2)}) collective-permute-start(bf16[1,32,1,16,128]{4,3,2,1,0:T(8,128)(2,1)S(1)} %get-tuple-element.6), channel_id=1, source_target_pairs={{0,1},{1,2},{2,3},{4,5},{5,6},{6,7},{8,9},{9,10},{10,11},{12,13},{... | collective-permute-start | bytes 393224 | tf_op jit(solution)/shard_map/ppermute | solution.py:17
  14.1 1.3 collective-permute-start.1
  15.4 3.4 %convert_reduce_fusion = f32[4096]{0:T(1024)S(1)} fusion(s32[1024]{0:T(1024)} %bitcast.152), kind=kLoop, calls=%fused_computation | loop fusion | flops 12578816 | bytes 20480 | tf_op jit(solution)/shard_map/reduce_sum | solution.py:53
  19.8 1.3 convolution_bitcast_fusion.1
  26.4 4.5 %copy.25 = bf16[32,27,2,16,128]{4,3,2,1,0:T(8,128)(2,1)} copy(bf16[32,27,2,16,128]{4,3,2,0,1:T(8,128)(2,1)S(1)} %fusion.49) | data formatting | bytes 14155776 | tf_op jit(solution)/shard_map/stack | solution.py:46
  31.7 12.1 %subtract_convert_fusion = (bf16[32,27,2,16,128]{4,3,2,0,1:T(8,128)(2,1)}, bf16[32,27,2,16,128]{4,3,2,0,1:T(8,128)(2,1)}) fusion(bf16[32,27,2,16,128]{4,3,2,0,1:T(8,128)(2,1)} %copy-done.1, f32[2,16,128]{2,1,0:T(8,128)S(1)} %bitcast.151), kind=kLoop, calls=%fused_computation.2 | loop fusion | flops 21233664 | bytes 21250048 | tf_op jit(solution)/shard_map/convert_element_type | solution.py:58
  43.8 7.1 %copy.26 = bf16[32,27,2,16,128]{4,3,2,1,0:T(8,128)(2,1)} copy(bf16[32,27,2,16,128]{4,3,2,0,1:T(8,128)(2,1)} %get-tuple-element.5) | data formatting | bytes 14155776 | tf_op jit(solution)/shard_map/convert_element_type | solution.py:57
  51.0 11.6 %convert_element_type.83 = bf16[864,4096]{1,0:T(8,128)(2,1)} reshape(bf16[32,27,2,16,128]{4,3,2,1,0:T(8,128)(2,1)} %copy.26) | data formatting | bytes 14155776 | tf_op jit(solution)/shard_map/convert_element_type | solution.py:57
  62.6 11.6 %reshape.94 = bf16[864,4096]{1,0:T(8,128)(2,1)} reshape(bf16[32,27,2,16,128]{4,3,2,1,0:T(8,128)(2,1)} %copy.25) | data formatting | bytes 14155776 | tf_op jit(solution)/shard_map/reshape | solution.py:46
  74.2 5.1 %convolution_bitcast_fusion = f32[32,864]{1,0:T(8,128)S(1)} fusion(bf16[864,4096]{1,0:T(8,128)(2,1)} %reshape.94, bf16[32,4096]{1,0:T(8,128)(2,1)S(1)} %reshape_squeeze.3), kind=kOutput, calls=%fused_computation.32 | convolution fusion | flops 226492416 | bytes 7450624 | tf_op jit(solution)/shard_map/dot_general | solution.py:50
  80.1 12.9 %fusion.60 = f32[864,864]{1,0:T(8,128)} fusion(bf16[864,4096]{1,0:T(8,128)(2,1)} %convert_element_type.83, bf16[864,4096]{1,0:T(8,128)(2,1)} %reshape.94), kind=kOutput, calls=%fused_computation.98 | convolution fusion | flops 6115295232 | bytes 17141760 | tf_op jit(solution)/shard_map/dot_general | solution.py:61
  93.0 7.0 %copy.27 = bf16[32,27,2,16,128]{4,3,2,1,0:T(8,128)(2,1)} copy(bf16[32,27,2,16,128]{4,3,2,0,1:T(8,128)(2,1)} %get-tuple-element.4) | data formatting | bytes 14155776 | tf_op jit(solution)/shard_map/convert_element_type | solution.py:58
  100.1 11.6 %convert_element_type.86 = bf16[864,4096]{1,0:T(8,128)(2,1)} reshape(bf16[32,27,2,16,128]{4,3,2,1,0:T(8,128)(2,1)} %copy.27) | data formatting | bytes 14155776 | tf_op jit(solution)/shard_map/convert_element_type | solution.py:58
  111.6 5.0 %all-reduce.6.cloned.1.call-done = f32[32,896]{1,0:T(8,128)} async-done(((f32[32,896]{1,0:T(8,128)}), f32[32,896]{1,0:T(8,128)}) %all-reduce.6.cloned.1.call-update) | async-done | bytes 114704 | tf_op jit(solution)/shard_map/psum | solution.py:6
  116.7 13.2 %multiply_convert_fusion = bf16[864,864]{1,0:T(8,128)(2,1)} fusion(f32[864,864]{1,0:T(8,128)} %fusion.60, bf16[864,4096]{1,0:T(8,128)(2,1)} %convert_element_type.86, bf16[864,4096]{1,0:T(8,128)(2,1)} %reshape.94), kind=kOutput, calls=%fused_computation.30 | convolution fusion | flops 6117534720 | bytes 18634752 | tf_op jit(solution)/shard_map/dot_general | solution.py:62
  129.9 4.6 %reshape.96 = bf16[8,108,4,216]{3,2,1,0:T(4,128)(2,1)S(1)} reshape(bf16[864,864]{1,0:T(8,128)(2,1)} %multiply_convert_fusion) | data formatting | bytes 2985984 | tf_op jit(solution)/shard_map/reshape | solution.py:68
  134.5 2.6 %copy.28 = bf16[8,4,108,216]{2,3,1,0:T(8,128)(2,1)} copy(bf16[8,4,108,216]{3,1,2,0:T(4,128)(2,1)S(1)} %bitcast.148) | data formatting | bytes 2985984 | tf_op jit(solution)/shard_map/transpose | solution.py:69
  137.2 4.3 %fusion.1 = bf16[4,8,32,128]{3,1,2,0:T(8,128)(2,1)S(1)} fusion(bf16[32,864]{1,0:T(8,128)(2,1)S(1)} %copy-done.2, bf16[864,4096]{1,0:T(8,128)(2,1)} %reshape.94), kind=kOutput, calls=%fused_computation.31 | convolution fusion | flops 226623488 | bytes 7395328 | tf_op jit(solution)/shard_map/dot_general | solution.py:48
  142.3 29.0 %all-reduce.8.cloned.1.call-done = f32[32,896]{1,0:T(8,128)} async-done(((f32[32,896]{1,0:T(8,128)}), f32[32,896]{1,0:T(8,128)}) %all-reduce.8.cloned.1.call-update) | async-done | bytes 114704 | tf_op jit(solution)/shard_map/psum | solution.py:6
  172.4 1.3 fusion.56
  173.7 1.4 slice.130
  175.1 52.1 %reduce-scatter.4.cloned.1.call-done = bf16[1,108,216]{1,2,0:T(8,128)(2,1)} async-done(((bf16[32,108,216]{1,2,0:T(8,128)(2,1)}), bf16[1,108,216]{1,2,0:T(8,128)(2,1)}) %reduce-scatter.4.cloned.1.call-update) | async-done | bytes 46672
  227.3 1.5 bitcast_convert_fusion
  228.7 1.6 copy.64
  (52 shorter events, 10.9 us)
Async XLA Ops:
  8.0 164.4 %copy-start = (f32[216,864]{1,0:T(8,128)S(1)}, f32[216,864]{1,0:T(8,128)}, u32[]{:S(2)}) copy-start(f32[216,864]{1,0:T(8,128)} %param.10) | copy-start | bytes 2239492
  8.0 108.6 %all-reduce.6.cloned.1.call-start = ((), (), s32[]{:S(2)}) async-start(), calls=%async_computation.1 | async-start | bytes 229376 | tf_op jit(solution)/shard_map/psum | solution.py:6
  9.1 12.0 %collective-permute-start = (bf16[1,32,1,16,128]{4,3,2,1,0:T(8,128)(2,1)S(1)}, bf16[1,32,1,16,128]{4,3,2,1,0:T(8,128)(2,1)S(1)}, u32[]{:S(2)}, u32[]{:S(2)}) collective-permute-start(bf16[1,32,1,16,128]{4,3,2,1,0:T(8,128)(2,1)S(1)} %get-tuple-element.6), channel_id=1, source_target_pairs={{0,1},{1,2},{2,3},{4,5},{5,6},{6,7},{8,9},{9,10},{10,11},{12,13},{... | collective-permute-start | bytes 393224 | tf_op jit(solution)/shard_map/ppermute | solution.py:17
  14.1 7.0 %collective-permute-start.1 = (bf16[1,32,1,16,128]{4,3,2,1,0:T(8,128)(2,1)S(1)}, bf16[1,32,1,16,128]{4,3,2,1,0:T(8,128)(2,1)S(1)}, u32[]{:S(2)}, u32[]{:S(2)}) collective-permute-start(bf16[1,32,1,16,128]{4,3,2,1,0:T(8,128)(2,1)S(1)} %get-tuple-element.7), channel_id=1, source_target_pairs={{1,0},{2,1},{3,2},{5,4},{6,5},{7,6},{9,8},{10,9},{11,10},{13,12},{... | collective-permute-start | bytes 393224 | tf_op jit(solution)/shard_map/ppermute | solution.py:19
  26.4 5.3 %copy-start.1 = (bf16[32,27,2,16,128]{4,3,2,0,1:T(8,128)(2,1)}, bf16[32,27,2,16,128]{4,3,2,0,1:T(8,128)(2,1)S(1)}, u32[]{:S(2)}) copy-start(bf16[32,27,2,16,128]{4,3,2,0,1:T(8,128)(2,1)S(1)} %fusion.49) | copy-start | bytes 21233668
  80.0 91.2 %all-reduce.8.cloned.1.call-start = ((), (), s32[]{:S(2)}) async-start(), calls=%async_computation.2 | async-start | bytes 229376 | tf_op jit(solution)/shard_map/psum | solution.py:6
  116.7 110.6 %reduce-scatter.4.cloned.1.call-start = ((), (), s32[]{:S(2)}) async-start(), calls=%async_computation.4 | async-start | bytes 1824768
  129.9 7.2 %copy-start.2 = (bf16[32,864]{1,0:T(8,128)(2,1)S(1)}, bf16[32,864]{1,0:T(8,128)(2,1)}, u32[]{:S(2)}) copy-start(bf16[32,864]{1,0:T(8,128)(2,1)} %param.8) | copy-start | bytes 165892
  134.5 36.8 %copy-start.3 = (f32[32,32]{1,0:T(8,128)S(1)}, f32[32,32]{1,0:T(8,128)}, u32[]{:S(2)}) copy-start(f32[32,32]{1,0:T(8,128)} %param.11) | copy-start | bytes 12292
  137.1 91.6 %all-reduce.10.cloned.1.call-start = ((), (), s32[]{:S(2)}) async-start(), calls=%async_computation.3 | async-start | bytes 229376 | tf_op jit(solution)/shard_map/psum | solution.py:80
Sparse Core Ops, SparseCore 0:
  80.2 36.4 all-reduce.5
  119.7 51.5 all-reduce.7
  174.3 35.3 all-reduce.9
Sparse Core Ops, SparseCore 1:
  137.2 90.0 reduce-scatter.3
